TPU v7x, 512 devices: a whole 4x8x8 slice. The times are simulated.
512 devices in a mesh: section: 8 (over y), expert: 32 (over z, x_hi, core), dp: 2 (over x_lo).
Axes of the slice: x: 4 (x_hi: 2, x_lo: 2; x = x_hi * 2 + x_lo), y: 8, z: 8, core: 2. Of those that a mesh axis runs over, the one named last changes fastest.
Arguments:
- blocks: bfloat16 [8, 512, 7168], P('section', ('expert', 'dp')), may hold values from -6 to 6
- gains: float32 [8, 7168], P('section'), may hold values from 0.1 to 1.9
- w_gate: bfloat16 [8, 7168, 4096], P('section', 'dp', 'expert'), may hold values from -0.0625 to 0.0625
- w_up: bfloat16 [8, 7168, 4096], P('section', 'dp', 'expert'), may hold values from -0.0625 to 0.0625
- w_down: bfloat16 [8, 7168, 4096], P('section', 'dp', 'expert'), may hold values from -0.1875 to 0.1875
- expert_ids: int32 [8, 2, 512, 2], P('section', None, ('expert', 'dp')), may hold values from 0 to 3, all different within a row; in each aligned block of 8 rows (0 to 7, 8 to 15, ..., all dimensions but the last counted through in order) at most 5 rows name the same one
- combine: float32 [8, 2, 512, 2], P('section', None, ('expert', 'dp')), may hold values from 0.2 to 1
Outputs:
- finished: bfloat16 [8, 512, 7168], P('section', ('expert', 'dp'))
Inputs may be any that keep to these rules, and one draw needn't show every extreme that they name: `expert_ids`: each token names 2 different experts; within the 8 tokens of one device (aligned blocks), no expert is named more than 5 times, a bound that some block reaches.
All inputs are finite; a program needn't handle non-finite values.
Results may differ from a plain program's by a relative error of at most 0.0073.
Values may be sent and summed in bfloat16 or wider, within the bound.
No kernel may reach another device: no remote copies, remote signals or barrier semaphores. Data moves between devices by JAX's collectives and lax.ppermute only.
A program may use at most 64 MiB of HBM per device.

v0:
```python
from functools import partial
import jax
import jax.numpy as jnp
from jax import lax
from jax.sharding import PartitionSpec as P


def passed_along(array, axis, by):
    length = lax.axis_size(axis)
    return lax.ppermute(array, axis, [(i, (i + by) % length) for i in range(length)])


def expert_rows(arrived, gate_full, up_full, down_full):
    sources, slot_count, model_width = arrived.shape
    flat_rows = arrived.reshape(sources * slot_count, model_width)
    gate_act = jnp.dot(flat_rows, gate_full, preferred_element_type=jnp.float32)
    upward = jnp.dot(flat_rows, up_full, preferred_element_type=jnp.float32)
    hidden = (jax.nn.silu(gate_act) * upward).astype(jnp.bfloat16)
    output = lax.dot_general(
        hidden, down_full, (((1,), (1,)), ((), ())), preferred_element_type=jnp.float32
    )
    output = output.astype(jnp.bfloat16).reshape(sources, slot_count, model_width)
    return lax.all_to_all(output, "expert", split_axis=0, concat_axis=0, tiled=True)


def moe_layer(stream, gain_row, weights, routes, mixing):
    owners = lax.axis_size("expert")
    experts = max(2, owners // 8)
    span = owners // experts
    tok_rows, model_width = stream.shape
    fan_out = routes.shape[1]
    capacity = min(tok_rows, max(2, 5 * tok_rows * fan_out // (4 * experts)))
    widened = stream.astype(jnp.float32)
    inv_rms = lax.rsqrt(jnp.mean(widened * widened, axis=1, keepdims=True) + 1e-06)
    normed = (widened * inv_rms * gain_row[None, :]).astype(jnp.bfloat16)
    flat_ids = routes.reshape(-1)
    count_all = flat_ids.shape[0]
    chosen = (flat_ids[:, None] == jnp.arange(experts, dtype=jnp.int32)[None, :]).astype(
        jnp.float32
    )
    triangle = (jnp.arange(count_all)[:, None] >= jnp.arange(count_all)[None, :]).astype(
        jnp.float32
    )
    running = jnp.dot(triangle, chosen, preferred_element_type=jnp.float32)
    slot_of = jnp.sum(chosen * (running - 1.0), axis=1).astype(jnp.int32)
    target = flat_ids * capacity + slot_of
    placing = jnp.arange(experts * capacity, dtype=jnp.int32)[:, None] == target[None, :]
    placing = (
        placing.reshape(experts * capacity, tok_rows, fan_out).any(axis=2).astype(jnp.bfloat16)
    )
    outgoing = jnp.dot(placing, normed, preferred_element_type=jnp.float32).astype(jnp.bfloat16)
    outgoing = jnp.repeat(outgoing.reshape(experts, capacity, model_width), span, axis=0)
    gate_full, up_full, down_full = weights
    worker = partial(expert_rows, gate_full=gate_full, up_full=up_full, down_full=down_full)
    returned = worker(lax.all_to_all(outgoing, "expert", split_axis=0, concat_axis=0, tiled=True))
    summed = jnp.sum(
        returned.reshape(experts, span, capacity, model_width).astype(jnp.float32), axis=1
    )
    expert_out = summed.astype(jnp.bfloat16).reshape(experts * capacity, model_width)
    picked = jnp.take(expert_out, target, axis=0)
    picked = picked.reshape(tok_rows, fan_out, model_width)
    mixed_sum = jnp.sum(mixing[:, :, None] * picked.astype(jnp.float32), axis=1)
    return (widened + mixed_sum).astype(jnp.bfloat16)


def on_device(blocks, gains, w_gate, w_up, w_down, expert_ids, combine):
    stream = blocks[0]
    turns = expert_ids.shape[1]
    weights = None
    for layer_turn in range(turns):
        if layer_turn > 0:
            stream = passed_along(stream, "section", 1)
        weights = (
            lax.all_gather(w_gate[0], "dp", axis=0, tiled=True),
            lax.all_gather(w_up[0], "dp", axis=0, tiled=True),
            lax.all_gather(w_down[0], "dp", axis=0, tiled=True),
        )
        stream = moe_layer(
            stream, gains[0], weights, expert_ids[0, layer_turn], combine[0, layer_turn]
        )
    return stream[None]


def solution(mesh):
    in_specs = (
        P("section", ("expert", "dp"), None),
        P("section", None),
        P("section", "dp", "expert"),
        P("section", "dp", "expert"),
        P("section", "dp", "expert"),
        P("section", None, ("expert", "dp"), None),
        P("section", None, ("expert", "dp"), None),
    )
    out_specs = P("section", ("expert", "dp"), None)
    return jax.shard_map(
        on_device, mesh=mesh, in_specs=in_specs, out_specs=out_specs, check_vma=False
    )
```

profile of v0, /device:TPU:32, one launch (start us, length us, event | category | flops | bytes accessed | tf_op | source)
XLA Modules:
  0.0 485.9 jit_solution(11815583365687878870)
XLA Ops:
  6.5 0.7 all-gather.7.cloned.1.call-update
  7.3 0.7 fusion.64
  8.9 0.7 bitcast_add_fusion.1
  9.7 1.1 fusion.34
  10.8 1.2 convolution_convert_fusion.3
  12.1 2.3 broadcast_in_dim.15
  14.4 13.3 %all-to-all-start = ((bf16[32,5,7168]{2,1,0:T(8,128)(2,1)}), bf16[32,5,7168]{2,1,0:T(8,128)(2,1)}, u32[]{:S(2)}, u32[]{:S(2)}) async-start(bf16[32,5,7168]{2,1,0:T(8,128)(2,1)} %bitcast.62), calls=%async_computation | async-start | bytes 7340032 | tf_op jit(solution)/shard_map/all_to_all | solution.py:55
  27.7 0.7 all-gather.11.cloned.1.call-update
  28.5 0.7 all-gather.9.cloned.1.call-update
  29.2 83.9 %all-to-all-done = bf16[32,5,7168]{2,1,0:T(8,128)(2,1)} async-done(((bf16[32,5,7168]{2,1,0:T(8,128)(2,1)}), bf16[32,5,7168]{2,1,0:T(8,128)(2,1)}, u32[]{:S(2)}, u32[]{:S(2)}) %all-to-all-start) | async-done | bytes 2293792 | tf_op jit(solution)/shard_map/all_to_all | solution.py:55
  113.1 3.3 reshape.115
  116.4 2.2 fusion.8
  118.7 41.1 %all-gather.9.cloned.1.call-done = bf16[1,7168,128]{2,1,0:T(8,128)(2,1)} async-done(((bf16[1,3584,128]{2,1,0:T(8,128)(2,1)}), bf16[1,7168,128]{2,1,0:T(8,128)(2,1)}) %all-gather.9.cloned.1.call-update) | async-done | bytes 1835024 | tf_op jit(solution)/shard_map/all_gather | solution.py:75
  159.8 4.9 %convolution_convert_fusion.1 = bf16[160,7168]{1,0:T(8,128)(2,1)} fusion(bf16[1,7168,128]{2,1,0:T(8,128)(2,1)} %all-gather.11.cloned.1.call-done, bf16[160,7168]{1,0:T(8,128)(2,1)S(1)} %reshape.115, bf16[1,7168,128]{2,1,0:T(8,128)(2,1)} %all-gather.9.cloned.1.call-done, f32[160,128]{1,0:T(8,128)S(1)} %fusion.8), kind=kOutput, calls=%fused_computation.3 | convolution fusion | flops 588472320 | bytes 8339456 | tf_op jit(solution)/shard_map/dot_general | solution.py:19
  164.6 4.6 reshape.116
  169.2 10.1 %all-to-all-start.1 = ((bf16[32,5,7168]{2,1,0:T(8,128)(2,1)}), bf16[32,5,7168]{2,1,0:T(8,128)(2,1)}, u32[]{:S(2)}, u32[]{:S(2)}) async-start(bf16[32,5,7168]{2,1,0:T(8,128)(2,1)} %reshape.116), calls=%async_computation.1 | async-start | bytes 7340032 | tf_op jit(solution)/shard_map/all_to_all | solution.py:23
  179.5 85.3 %all-to-all-done.1 = bf16[32,5,7168]{2,1,0:T(8,128)(2,1)} async-done(((bf16[32,5,7168]{2,1,0:T(8,128)(2,1)}), bf16[32,5,7168]{2,1,0:T(8,128)(2,1)}, u32[]{:S(2)}, u32[]{:S(2)}) %all-to-all-start.1) | async-done | bytes 2293792 | tf_op jit(solution)/shard_map/all_to_all | solution.py:23
  264.8 2.8 bitcast_reduce_fusion.1
  267.7 0.7 gather_fusion
  268.8 0.6 multiply_reduce_fusion.1
  269.5 2.5 collective-permute-start
  272.1 5.3 %collective-permute-done = bf16[8,7168]{1,0:T(8,128)(2,1)S(1)} collective-permute-done((bf16[8,7168]{1,0:T(8,128)(2,1)S(1)}, bf16[8,7168]{1,0:T(8,128)(2,1)S(1)}, u32[]{:S(2)}, u32[]{:S(2)}) %collective-permute-start) | collective-permute-done | bytes 114720 | tf_op jit(solution)/shard_map/ppermute | solution.py:10
  278.4 90.5 %all_to_all.20 = bf16[32,5,7168]{2,1,0:T(8,128)(2,1)} all-to-all(bf16[32,5,7168]{2,1,0:T(8,128)(2,1)S(1)} %bitcast.63), channel_id=1, replica_groups=mesh['section'=8,'expert'=32,'dp'=2] {'expert'}, dimensions={0} | all-to-all | bytes 4587520 | tf_op jit(solution)/shard_map/all_to_all | solution.py:55
  368.9 3.3 reshape.121
  372.2 2.2 fusion.6
  374.4 4.9 %convolution_convert_fusion = bf16[160,7168]{1,0:T(8,128)(2,1)} fusion(bf16[1,7168,128]{2,1,0:T(8,128)(2,1)} %all-gather.11.cloned.1.call-done, bf16[160,7168]{1,0:T(8,128)(2,1)S(1)} %reshape.121, bf16[1,7168,128]{2,1,0:T(8,128)(2,1)} %all-gather.9.cloned.1.call-done, f32[160,128]{1,0:T(8,128)S(1)} %fusion.6), kind=kOutput, calls=%fused_computation.2 | convolution fusion | flops 588472320 | bytes 8339456 | tf_op jit(solution)/shard_map/dot_general | solution.py:19
  379.3 4.6 reshape.122
  383.9 4.8 all-to-all-start.3
  388.8 85.3 %all-to-all-done.3 = bf16[32,5,7168]{2,1,0:T(8,128)(2,1)} async-done(((bf16[32,5,7168]{2,1,0:T(8,128)(2,1)}), bf16[32,5,7168]{2,1,0:T(8,128)(2,1)}, u32[]{:S(2)}, u32[]{:S(2)}) %all-to-all-start.3) | async-done | bytes 2293792 | tf_op jit(solution)/shard_map/all_to_all | solution.py:23
  474.1 2.8 bitcast_reduce_fusion
  477.0 0.7 gather_fusion.1
  478.7 0.7 fusion.39
  (47 shorter events, 4.3 us)
Async XLA Ops:
  6.5 109.9 %all-gather.7.cloned.1.call-start = ((), (), s32[]{:S(2)}) async-start(), calls=%async_computation.4 | async-start | bytes 2752512 | tf_op jit(solution)/shard_map/all_gather | solution.py:74
  14.4 98.7 %all-to-all-start = ((bf16[32,5,7168]{2,1,0:T(8,128)(2,1)}), bf16[32,5,7168]{2,1,0:T(8,128)(2,1)}, u32[]{:S(2)}, u32[]{:S(2)}) async-start(bf16[32,5,7168]{2,1,0:T(8,128)(2,1)} %bitcast.62), calls=%async_computation | async-start | bytes 7340032 | tf_op jit(solution)/shard_map/all_to_all | solution.py:55
  27.7 91.0 %all-gather.11.cloned.1.call-start = ((), (), s32[]{:S(2)}) async-start(), calls=%async_computation.6 | async-start | bytes 2752512 | tf_op jit(solution)/shard_map/all_gather | solution.py:76
  28.4 131.3 %all-gather.9.cloned.1.call-start = ((), (), s32[]{:S(2)}) async-start(), calls=%async_computation.5 | async-start | bytes 2752512 | tf_op jit(solution)/shard_map/all_gather | solution.py:75
  169.2 10.1 %copy-start.2 = (f32[1,2,8,2]{2,3,1,0:T(2,128)S(1)}, f32[1,2,8,2]{2,3,1,0:T(2,128)}, u32[]{:S(2)}) copy-start(f32[1,2,8,2]{2,3,1,0:T(2,128)} %param.15) | copy-start | bytes 388
  169.2 95.6 %all-to-all-start.1 = ((bf16[32,5,7168]{2,1,0:T(8,128)(2,1)}), bf16[32,5,7168]{2,1,0:T(8,128)(2,1)}, u32[]{:S(2)}, u32[]{:S(2)}) async-start(bf16[32,5,7168]{2,1,0:T(8,128)(2,1)} %reshape.116), calls=%async_computation.1 | async-start | bytes 7340032 | tf_op jit(solution)/shard_map/all_to_all | solution.py:23
  267.7 1.7 copy-start
  267.7 9.9 %copy-start.1 = (f32[1,7168]{1,0:T(1,128)S(1)}, f32[1,7168]{1,0:T(1,128)}, u32[]{:S(2)}) copy-start(f32[1,7168]{1,0:T(1,128)} %param.10) | copy-start | bytes 86020
  269.5 7.9 %collective-permute-start = (bf16[8,7168]{1,0:T(8,128)(2,1)S(1)}, bf16[8,7168]{1,0:T(8,128)(2,1)S(1)}, u32[]{:S(2)}, u32[]{:S(2)}) collective-permute-start(bf16[8,7168]{1,0:T(8,128)(2,1)S(1)} %fusion.37), channel_id=1, source_target_pairs={{0,64},{64,128},{128,192},{192,256},{256,320},{320,384},{384,448},... | collective-permute-start | bytes 344072 | tf_op jit(solution)/shard_map/ppermute | solution.py:10
  383.9 90.2 %all-to-all-start.3 = ((bf16[32,5,7168]{2,1,0:T(8,128)(2,1)}), bf16[32,5,7168]{2,1,0:T(8,128)(2,1)}, u32[]{:S(2)}, u32[]{:S(2)}) async-start(bf16[32,5,7168]{2,1,0:T(8,128)(2,1)} %reshape.122), calls=%async_computation.3 | async-start | bytes 7340032 | tf_op jit(solution)/shard_map/all_to_all | solution.py:23
Sparse Core Ops, SparseCore 0:
  9.4 63.5 all-gather.6
  75.1 42.5 all-gather.10
  119.8 39.9 all-gather.8
where the time goes:
time: 487 us; the launch traced here: 486 us
  waiting for transfers between devices  303 us (62%)
  blocking collectives  90.5 us (19%)
  starting transfers between devices  30.8 us (6%)
  local copies, waits for them, and re-layouts  22.2 us (5%)
  matrix products  16 us (3%)
  between operations  13.4 us (3%)
  other arithmetic  9.93 us (2%)
    all_to_all x2, waiting for transfers between devices, expert_rows(): lax.all_to_all(output, 'expert', split_axis=0, concat_axis=0, tiled=True)  171 us
    all_to_all x1, blocking collectives, moe_layer(): lax.all_to_all(outgoing, 'expert', split_axis=0, concat_axis=0, tiled=True)  90.5 us
    all_to_all x1, waiting for transfers between devices, moe_layer(): lax.all_to_all(outgoing, 'expert', split_axis=0, concat_axis=0, tiled=True)  83.9 us
    all_gather x1, waiting for transfers between devices, on_device(): lax.all_gather(w_up[0], 'dp', axis=0, tiled=True)  41.1 us
    all_to_all x2, starting transfers between devices, expert_rows(): lax.all_to_all(output, 'expert', split_axis=0, concat_axis=0, tiled=True)  15 us
    all_to_all x1, starting transfers between devices, moe_layer(): lax.all_to_all(outgoing, 'expert', split_axis=0, concat_axis=0, tiled=True)  13.3 us
    dot_general x2, matrix products, expert_rows(): lax.dot_general(hidden, down_full, (((1,), (1,)), ((), ())), preferred_el...  9.76 us
  transfers between devices with their start and end apart: 7, of which 5 were waited for; matrix products, arithmetic and copies ran while one was open for 3% of the time, Pallas kernels for 0%

commit v1 on v0

--- a/solution.py
+++ b/solution.py
@@ -3,6 +3,16 @@
 import jax.numpy as jnp
 from jax import lax
 from jax.sharding import PartitionSpec as P
+
+
+def store_words(mesh_dim, values):
+    val2 = jnp.concatenate(
+        lax.all_to_all(
+            jnp.stack([values for _ in range(lax.axis_size(mesh_dim))], 0), mesh_dim, 0, 0
+        ),
+        0,
+    )
+    return val2
 
 
 def passed_along(array, axis, by):
@@ -72,7 +82,7 @@
             stream = passed_along(stream, "section", 1)
         weights = (
             lax.all_gather(w_gate[0], "dp", axis=0, tiled=True),
-            lax.all_gather(w_up[0], "dp", axis=0, tiled=True),
+            store_words("dp", w_up[0]),
             lax.all_gather(w_down[0], "dp", axis=0, tiled=True),
         )
         stream = moe_layer(

time: 487 us -> 472 us (0.969)
  waiting for transfers between devices: 303 us -> 281 us
    all_gather x1 -> x0, waiting for transfers between devices: 41.1 us -> none  [on_device(): lax.all_gather(w_up[0], 'dp', axis=0, tiled=True)]
    all_to_all x0 -> x1, waiting for transfers between devices: none -> 21.7 us  [store_words(): lax.all_to_all(jnp.stack([values for _ in range(lax.axis_size(mesh_dim))]...]
  transfers between devices with their start and end apart: 7 -> 7, of which waited for: 5 -> 5; matrix products, arithmetic and copies ran while one was open for 3% -> 2% of each run, Pallas kernels for 0% -> 0%
where the time goes in v1:
time: 472 us; the launch traced here: 471 us
  waiting for transfers between devices  281 us (60%)
  blocking collectives  90.5 us (19%)
  starting transfers between devices  35.5 us (8%)
  local copies, waits for them, and re-layouts  22.2 us (5%)
  matrix products  16.1 us (3%)
  between operations  13.7 us (3%)
  other arithmetic  11.4 us (2%)
    all_to_all x2, waiting for transfers between devices, expert_rows(): lax.all_to_all(output, 'expert', split_axis=0, concat_axis=0, tiled=True)  171 us
    all_to_all x1, blocking collectives, moe_layer(): lax.all_to_all(outgoing, 'expert', split_axis=0, concat_axis=0, tiled=True)  90.5 us
    all_to_all x1, waiting for transfers between devices, moe_layer(): lax.all_to_all(outgoing, 'expert', split_axis=0, concat_axis=0, tiled=True)  82.5 us
    all_to_all x1, waiting for transfers between devices, store_words(): lax.all_to_all(jnp.stack([values for _ in range(lax.axis_size(mesh_dim))]...  21.7 us
    all_to_all x2, starting transfers between devices, expert_rows(): lax.all_to_all(output, 'expert', split_axis=0, concat_axis=0, tiled=True)  15 us
    all_to_all x1, starting transfers between devices, moe_layer(): lax.all_to_all(outgoing, 'expert', split_axis=0, concat_axis=0, tiled=True)  13.3 us
    dot_general x2, matrix products, expert_rows(): lax.dot_general(hidden, down_full, (((1,), (1,)), ((), ())), preferred_el...  9.76 us
  transfers between devices with their start and end apart: 7, of which 5 were waited for; matrix products, arithmetic and copies ran while one was open for 2% of the time, Pallas kernels for 0%

profile of v1, /device:TPU:32, one launch (start us, length us, event | category | flops | bytes accessed | tf_op | source)
XLA Modules:
  0.0 470.8 jit_solution(12169627539251073792)
XLA Ops:
  6.5 0.7 fusion.46
  8.2 0.7 bitcast_add_fusion.1
  9.0 1.1 fusion.16
  10.1 1.2 convolution_convert_fusion.3
  11.4 2.3 broadcast_in_dim.15
  13.7 13.3 %all-to-all-start = ((bf16[32,5,7168]{2,1,0:T(8,128)(2,1)}), bf16[32,5,7168]{2,1,0:T(8,128)(2,1)}, u32[]{:S(2)}, u32[]{:S(2)}) async-start(bf16[32,5,7168]{2,1,0:T(8,128)(2,1)} %bitcast.48), calls=%async_computation | async-start | bytes 7340032 | tf_op jit(solution)/shard_map/all_to_all | solution.py:65
  27.0 0.7 all-gather.5.cloned.1.call-update
  27.8 0.7 all-gather.7.cloned.1.call-update
  28.5 1.4 pad_maximum_fusion
  29.9 82.5 %all-to-all-done = bf16[32,5,7168]{2,1,0:T(8,128)(2,1)} async-done(((bf16[32,5,7168]{2,1,0:T(8,128)(2,1)}), bf16[32,5,7168]{2,1,0:T(8,128)(2,1)}, u32[]{:S(2)}, u32[]{:S(2)}) %all-to-all-start) | async-done | bytes 2293792 | tf_op jit(solution)/shard_map/all_to_all | solution.py:65
  112.4 4.7 %all-to-all-start.1 = ((bf16[2,3584,128]{2,1,0:T(8,128)(2,1)}), bf16[2,3584,128]{2,1,0:T(8,128)(2,1)}, u32[]{:S(2)}, u32[]{:S(2)}) async-start(bf16[2,3584,128]{2,1,0:T(8,128)(2,1)} %pad_maximum_fusion), calls=%async_computation.1 | async-start | bytes 3670016 | tf_op jit(solution)/shard_map/all_to_all | solution.py:10
  117.1 3.3 reshape.119
  120.4 2.2 fusion.4
  122.7 21.7 %all-to-all-done.1 = bf16[2,3584,128]{2,1,0:T(8,128)(2,1)} async-done(((bf16[2,3584,128]{2,1,0:T(8,128)(2,1)}), bf16[2,3584,128]{2,1,0:T(8,128)(2,1)}, u32[]{:S(2)}, u32[]{:S(2)}) %all-to-all-start.1) | async-done | bytes 1835040 | tf_op jit(solution)/shard_map/all_to_all | solution.py:10
  144.3 4.9 %convolution_convert_fusion.1 = bf16[160,7168]{1,0:T(8,128)(2,1)} fusion(bf16[1,7168,128]{2,1,0:T(8,128)(2,1)} %all-gather.7.cloned.1.call-done, bf16[160,7168]{1,0:T(8,128)(2,1)S(1)} %reshape.119, bf16[7168,128]{1,0:T(8,128)(2,1)} %bitcast.7, f32[160,128]{1,0:T(8,128)S(1)} %fusion.4), kind=kOutput, calls=%fused_computation.3 | convolution fusion | flops 588472320 | bytes 8339456 | tf_op jit(solution)/shard_map/dot_general | solution.py:29
  149.2 4.6 reshape.121
  153.8 10.1 %all-to-all-start.2 = ((bf16[32,5,7168]{2,1,0:T(8,128)(2,1)}), bf16[32,5,7168]{2,1,0:T(8,128)(2,1)}, u32[]{:S(2)}, u32[]{:S(2)}) async-start(bf16[32,5,7168]{2,1,0:T(8,128)(2,1)} %reshape.121), calls=%async_computation.2 | async-start | bytes 7340032 | tf_op jit(solution)/shard_map/all_to_all | solution.py:33
  164.0 85.3 %all-to-all-done.2 = bf16[32,5,7168]{2,1,0:T(8,128)(2,1)} async-done(((bf16[32,5,7168]{2,1,0:T(8,128)(2,1)}), bf16[32,5,7168]{2,1,0:T(8,128)(2,1)}, u32[]{:S(2)}, u32[]{:S(2)}) %all-to-all-start.2) | async-done | bytes 2293792 | tf_op jit(solution)/shard_map/all_to_all | solution.py:33
  249.3 2.8 bitcast_reduce_fusion.1
  252.3 0.7 gather_fusion
  254.1 2.5 collective-permute-start
  256.6 5.3 %collective-permute-done = bf16[8,7168]{1,0:T(8,128)(2,1)S(1)} collective-permute-done((bf16[8,7168]{1,0:T(8,128)(2,1)S(1)}, bf16[8,7168]{1,0:T(8,128)(2,1)S(1)}, u32[]{:S(2)}, u32[]{:S(2)}) %collective-permute-start) | collective-permute-done | bytes 114720 | tf_op jit(solution)/shard_map/ppermute | solution.py:20
  263.0 90.5 %all_to_all.26 = bf16[32,5,7168]{2,1,0:T(8,128)(2,1)} all-to-all(bf16[32,5,7168]{2,1,0:T(8,128)(2,1)S(1)} %bitcast.49), channel_id=1, replica_groups=mesh['section'=8,'expert'=32,'dp'=2] {'expert'}, dimensions={0} | all-to-all | bytes 4587520 | tf_op jit(solution)/shard_map/all_to_all | solution.py:65
  353.5 3.3 reshape.126
  356.7 2.2 fusion.2
  359.0 4.9 %convolution_convert_fusion = bf16[160,7168]{1,0:T(8,128)(2,1)} fusion(bf16[1,7168,128]{2,1,0:T(8,128)(2,1)} %all-gather.7.cloned.1.call-done, bf16[160,7168]{1,0:T(8,128)(2,1)S(1)} %reshape.126, bf16[7168,128]{1,0:T(8,128)(2,1)} %bitcast.7, f32[160,128]{1,0:T(8,128)S(1)} %fusion.2), kind=kOutput, calls=%fused_computation.2 | convolution fusion | flops 588472320 | bytes 8339456 | tf_op jit(solution)/shard_map/dot_general | solution.py:29
  363.9 4.6 reshape.127
  368.4 4.8 %all-to-all-start.4 = ((bf16[32,5,7168]{2,1,0:T(8,128)(2,1)}), bf16[32,5,7168]{2,1,0:T(8,128)(2,1)}, u32[]{:S(2)}, u32[]{:S(2)}) async-start(bf16[32,5,7168]{2,1,0:T(8,128)(2,1)} %reshape.127), calls=%async_computation.4 | async-start | bytes 7340032 | tf_op jit(solution)/shard_map/all_to_all | solution.py:33
  373.4 85.3 %all-to-all-done.4 = bf16[32,5,7168]{2,1,0:T(8,128)(2,1)} async-done(((bf16[32,5,7168]{2,1,0:T(8,128)(2,1)}), bf16[32,5,7168]{2,1,0:T(8,128)(2,1)}, u32[]{:S(2)}, u32[]{:S(2)}) %all-to-all-start.4) | async-done | bytes 2293792 | tf_op jit(solution)/shard_map/all_to_all | solution.py:33
  458.7 2.8 bitcast_reduce_fusion
  461.6 0.7 gather_fusion.1
  463.3 0.7 fusion.21
  (49 shorter events, 4.9 us)
Async XLA Ops:
  13.7 98.7 %all-to-all-start = ((bf16[32,5,7168]{2,1,0:T(8,128)(2,1)}), bf16[32,5,7168]{2,1,0:T(8,128)(2,1)}, u32[]{:S(2)}, u32[]{:S(2)}) async-start(bf16[32,5,7168]{2,1,0:T(8,128)(2,1)} %bitcast.48), calls=%async_computation | async-start | bytes 7340032 | tf_op jit(solution)/shard_map/all_to_all | solution.py:65
  27.0 1.5 copy-start.1
  27.0 93.4 %all-gather.5.cloned.1.call-start = ((), (), s32[]{:S(2)}) async-start(), calls=%async_computation.5 | async-start | bytes 2752512 | tf_op jit(solution)/shard_map/all_gather | solution.py:84
  27.7 116.6 %all-gather.7.cloned.1.call-start = ((), (), s32[]{:S(2)}) async-start(), calls=%async_computation.6 | async-start | bytes 2752512 | tf_op jit(solution)/shard_map/all_gather | solution.py:86
  112.4 31.9 %all-to-all-start.1 = ((bf16[2,3584,128]{2,1,0:T(8,128)(2,1)}), bf16[2,3584,128]{2,1,0:T(8,128)(2,1)}, u32[]{:S(2)}, u32[]{:S(2)}) async-start(bf16[2,3584,128]{2,1,0:T(8,128)(2,1)} %pad_maximum_fusion), calls=%async_computation.1 | async-start | bytes 3670016 | tf_op jit(solution)/shard_map/all_to_all | solution.py:10
  153.8 10.2 %copy-start.3 = (f32[1,2,8,2]{2,3,1,0:T(2,128)S(1)}, f32[1,2,8,2]{2,3,1,0:T(2,128)}, u32[]{:S(2)}) copy-start(f32[1,2,8,2]{2,3,1,0:T(2,128)} %param.15) | copy-start | bytes 388
  153.8 95.6 %all-to-all-start.2 = ((bf16[32,5,7168]{2,1,0:T(8,128)(2,1)}), bf16[32,5,7168]{2,1,0:T(8,128)(2,1)}, u32[]{:S(2)}, u32[]{:S(2)}) async-start(bf16[32,5,7168]{2,1,0:T(8,128)(2,1)} %reshape.121), calls=%async_computation.2 | async-start | bytes 7340032 | tf_op jit(solution)/shard_map/all_to_all | solution.py:33
  252.3 1.7 copy-start
  252.3 9.9 %copy-start.2 = (f32[1,7168]{1,0:T(1,128)S(1)}, f32[1,7168]{1,0:T(1,128)}, u32[]{:S(2)}) copy-start(f32[1,7168]{1,0:T(1,128)} %param.10) | copy-start | bytes 86020
  254.1 7.9 %collective-permute-start = (bf16[8,7168]{1,0:T(8,128)(2,1)S(1)}, bf16[8,7168]{1,0:T(8,128)(2,1)S(1)}, u32[]{:S(2)}, u32[]{:S(2)}) collective-permute-start(bf16[8,7168]{1,0:T(8,128)(2,1)S(1)} %fusion.19), channel_id=1, source_target_pairs={{0,64},{64,128},{128,192},{192,256},{256,320},{320,384},{384,448},... | collective-permute-start | bytes 344072 | tf_op jit(solution)/shard_map/ppermute | solution.py:20
  368.4 90.2 %all-to-all-start.4 = ((bf16[32,5,7168]{2,1,0:T(8,128)(2,1)}), bf16[32,5,7168]{2,1,0:T(8,128)(2,1)}, u32[]{:S(2)}, u32[]{:S(2)}) async-start(bf16[32,5,7168]{2,1,0:T(8,128)(2,1)} %reshape.127), calls=%async_computation.4 | async-start | bytes 7340032 | tf_op jit(solution)/shard_map/all_to_all | solution.py:33
Sparse Core Ops, SparseCore 0:
  29.9 49.2 all-gather.4
  81.3 49.4 all-gather.6
